TPU v7x, 32 devices: a whole 2x2x4 slice. The times are simulated.
32 devices in a mesh: mol: 2 (over x), occ: 16 (over z, y, core).
Axes of the slice: x: 2, y: 2, z: 4, core: 2. Of those that a mesh axis runs over, the one named last changes fastest.
Arguments:
- integrals: bfloat16 [512, 128, 2048], P(('mol', 'occ')), parts along dimension 0, may hold values from -6 to 6
- orbitals: bfloat16 [4096, 1536], P('mol'), parts along dimension 0
- occ_energy: float32 [256], P('mol'), parts along dimension 0, may hold values from -2 to -0.3
- vir_energy: float32 [3072], P('mol'), parts along dimension 0, may hold values from 0.1 to 3
- owner: int32 [16], P('mol'), parts along dimension 0, may hold values from 0 to 127
- vblock: int32 [16], P('mol'), parts along dimension 0, may hold values from 0 to 7
Outputs:
- factors: bfloat16 [512, 128, 1536], P('mol', 'occ'), parts along dimension 0
- pair_energy: float32 [256, 8], P(('mol', 'occ')), parts along dimension 0
There are 2 independent parts, one for each index of `mol`. A program takes and returns all parts, laid end to end along the dimension named above; each array names one. Nothing has to cross between parts.
Inputs may be any that keep to these rules, and one draw needn't show every extreme that they name: `owner`: each step names one occupied orbital and one virtual block; steps may repeat.
All inputs are finite; a program needn't handle non-finite values.
Results may differ from a plain program's by a relative error of at most 0.001.
Values may be sent and summed in bfloat16 or wider, within the bound.
No kernel may reach another device: no remote copies, remote signals or barrier semaphores. Data moves between devices by JAX's collectives and lax.ppermute only.
A program may use at most 128 MiB of HBM per device.

v0:
```python
import jax
import jax.numpy as jnp
from jax import lax
from jax.sharding import PartitionSpec as P

VBLK = 192


def pair_column(factors, block, occ_here, occ_energy, vir_energy, orbital_j, block_id):
    coulomb = lax.dot_general(
        factors, block, (((0,), (0,)), ((), ())), preferred_element_type=jnp.float32
    )
    vir_block = lax.dynamic_slice(vir_energy, (block_id * VBLK,), (VBLK,))
    occ_j = occ_energy[orbital_j]
    denom = vir_energy[None, :, None] + vir_block[None, None, :] - occ_here[:, None, None] - occ_j
    scale = 1.0 / (factors.shape[0] * vir_energy.shape[0] * VBLK)
    return -jnp.sum(coulomb * coulomb / denom, axis=(1, 2)) * scale


def per_device(integrals, orbitals, occ_energy, vir_energy, owner, vblock):
    aux_here, occ_total, basis_count = integrals.shape
    step_count = owner.shape[0]
    flat = integrals.reshape(aux_here * occ_total, basis_count)
    product = jnp.dot(flat, orbitals, preferred_element_type=jnp.float32).astype(jnp.bfloat16)
    product = product.reshape(aux_here, occ_total, orbitals.shape[1])

    def own_piece(step):
        piece = lax.dynamic_slice(
            product, (jnp.int32(0), owner[step], vblock[step] * VBLK), (aux_here, 1, VBLK)
        )
        return piece[:, 0, :]

    pieces = jnp.stack([own_piece(step) for step in range(step_count)], axis=1)
    blocks = lax.all_gather(pieces, "occ", axis=0, tiled=True)
    factors = lax.all_to_all(product, "occ", split_axis=1, concat_axis=0, tiled=True)
    local_count = factors.shape[1]
    occ_here = lax.dynamic_slice(occ_energy, (lax.axis_index("occ") * local_count,), (local_count,))
    energies = jnp.zeros((local_count, step_count), jnp.float32)

    def step_body(step, energies):
        orbital_j = owner[step]
        block_id = vblock[step]
        block = lax.dynamic_index_in_dim(blocks, step, axis=1, keepdims=False)
        column = pair_column(factors, block, occ_here, occ_energy, vir_energy, orbital_j, block_id)
        return lax.dynamic_update_slice(energies, column[:, None], (jnp.int32(0), step))

    energies = lax.fori_loop(0, step_count, step_body, energies)
    return (factors, energies)


def solution(mesh):
    placed = (P(("mol", "occ"), None, None), P("mol", None), P("mol"), P("mol"), P("mol"), P("mol"))
    return jax.shard_map(
        per_device,
        mesh=mesh,
        in_specs=placed,
        out_specs=(P("mol", "occ", None), P(("mol", "occ"), None)),
        check_vma=False,
    )
```

profile of v0, /device:TPU:9, one launch (start us, length us, event | category | flops | bytes accessed | tf_op | source)
XLA Modules:
  0.0 285.7 jit_solution(6650717841820332586)
XLA Ops:
  0.6 17.3 %convolution_convert_fusion = bf16[2048,1536]{1,0:T(8,128)(2,1)S(1)} fusion(bf16[2048,2048]{1,0:T(8,128)(2,1)} %bitcast.56, bf16[2048,1536]{1,0:T(8,128)(2,1)} %param.9), kind=kOutput, calls=%fused_computation.7 | convolution fusion | flops 12888047616 | bytes 20971520 | tf_op jit(solution)/shard_map/dot_general | solution.py:24
  17.9 2.6 copy-done.1
  20.5 6.2 %copy.19 = bf16[16,128,1536]{2,0,1:T(8,128)(2,1)} copy(bf16[16,128,1536]{2,1,0:T(8,128)(2,1)S(1)} %bitcast.54) | data formatting | bytes 12582912 | tf_op jit(solution)/shard_map/reshape | solution.py:25
  26.8 6.7 %all-to-all-start = ((bf16[16,128,1536]{2,0,1:T(8,128)(2,1)}), bf16[16,128,1536]{2,0,1:T(8,128)(2,1)}, u32[]{:S(2)}, u32[]{:S(2)}) async-start(bf16[16,128,1536]{2,0,1:T(8,128)(2,1)} %copy.19), calls=%async_computation | async-start | bytes 12582912 | tf_op jit(solution)/shard_map/all_to_all | solution.py:35
  33.5 0.7 fusion.4
  39.2 0.7 fusion.5
  55.2 1.5 constant_dynamic-slice_fusion
  56.8 0.2 stack.3
  57.0 127.9 %all_gather.3 = bf16[256,8,192]{2,1,0:T(8,128)(2,1)S(1)} all-gather(bf16[16,8,192]{2,1,0:T(8,128)(2,1)S(1)} %stack.3), channel_id=1, replica_groups=mesh['mol'=2,'occ'=16] {'occ'}, dimensions={0}, use_global_device_ids=true | all-gather | bytes 835584 | tf_op jit(solution)/shard_map/all_gather | solution.py:34
  184.8 1.0 copy.21
  185.9 0.1 dynamic_slice.71
  185.9 6.9 %copy.20 = bf16[16,16,8,1536]{3,2,1,0:T(8,128)(2,1)S(1)} copy(bf16[16,16,8,1536]{3,1,2,0:T(8,128)(2,1)} %bitcast.10) | data formatting | bytes 12582912 | tf_op jit(solution)/shard_map/all_to_all | solution.py:35
  192.8 0.0 copy-start.2
  192.9 4.7 %copy.22 = bf16[256,8,1536]{2,0,1:T(8,128)(2,1)} copy(bf16[256,8,1536]{2,1,0:T(8,128)(2,1)S(1)} %bitcast.52) | data formatting | bytes 12582912 | tf_op jit(solution)/shard_map/while | solution.py:47
  197.6 87.4 %while.13 = (s32[]{:T(128)}, f32[8,8]{0,1:T(8,128)S(1)}, bf16[256,8,192]{0,2,1:T(8,128)(2,1)S(1)}, bf16[256,8,1536]{2,0,1:T(8,128)(2,1)}, f32[1536]{0:T(1024)S(1...) while((s32[]{:T(128)}, f32[8,8]{0,1:T(8,128)S(1)}, ...), condition=%wide.region_2.3_spmd, body=%wide.region_0.2_spmd.sunk | while | flops 1220050944 | bytes 8758441 | solution.py:47
  197.6 0.6 dynamic_slice.92
  198.8 0.1 dynamic_slice.93
  198.9 0.1 broadcast_add_fusion.2
  199.1 0.6 dynamic_slice.90
  201.6 0.6 dynamic_slice.91
  202.2 6.3 %fusion.14 = f32[8]{0:T(128)S(1)} fusion(bf16[256,8,1536]{2,0,1:T(8,128)(2,1)} %get-tuple-element.307, f32[]{:T(128)} %bitcast.50, f32[8]{0:T(128)S(1)} %get-tuple-element.310, f32[1536,192]{0,1:T(8,128)S(1)} %broadcast_add_fusion.2, bf16[256,8,192]{0,2,1:T(8,128)(2,1)S(1)} %get-tuple-element.306, s32[]{:T(128)} %get-tuple-element.290), kind=kOutput, calls=%fused_computation.1.clone.1 | convolution fusion | flops 1219756032 | bytes 7569960 | tf_op jit(solution)/shard_map/while/body/eval_jaxpr/dot_general | solution.py:10
  208.5 0.6 dynamic_slice.92
  209.8 0.1 dynamic_slice.93
  209.8 0.1 broadcast_add_fusion.2
  210.0 0.6 dynamic_slice.90
  212.5 0.6 dynamic_slice.91
  213.1 6.3 %fusion.14 = f32[8]{0:T(128)S(1)} fusion(bf16[256,8,1536]{2,0,1:T(8,128)(2,1)} %get-tuple-element.307, f32[]{:T(128)} %bitcast.50, f32[8]{0:T(128)S(1)} %get-tuple-element.310, f32[1536,192]{0,1:T(8,128)S(1)} %broadcast_add_fusion.2, bf16[256,8,192]{0,2,1:T(8,128)(2,1)S(1)} %get-tuple-element.306, s32[]{:T(128)} %get-tuple-element.290), kind=kOutput, calls=%fused_computation.1.clone.1 | convolution fusion | flops 1219756032 | bytes 7569960 | tf_op jit(solution)/shard_map/while/body/eval_jaxpr/dot_general | solution.py:10
  219.4 0.6 dynamic_slice.92
  220.7 0.1 dynamic_slice.93
  220.8 0.1 broadcast_add_fusion.2
  220.9 0.6 dynamic_slice.90
  223.5 0.6 dynamic_slice.91
  224.1 6.3 %fusion.14 = f32[8]{0:T(128)S(1)} fusion(bf16[256,8,1536]{2,0,1:T(8,128)(2,1)} %get-tuple-element.307, f32[]{:T(128)} %bitcast.50, f32[8]{0:T(128)S(1)} %get-tuple-element.310, f32[1536,192]{0,1:T(8,128)S(1)} %broadcast_add_fusion.2, bf16[256,8,192]{0,2,1:T(8,128)(2,1)S(1)} %get-tuple-element.306, s32[]{:T(128)} %get-tuple-element.290), kind=kOutput, calls=%fused_computation.1.clone.1 | convolution fusion | flops 1219756032 | bytes 7569960 | tf_op jit(solution)/shard_map/while/body/eval_jaxpr/dot_general | solution.py:10
  230.4 0.6 dynamic_slice.92
  231.6 0.1 dynamic_slice.93
  231.7 0.1 broadcast_add_fusion.2
  231.9 0.6 dynamic_slice.90
  234.4 0.6 dynamic_slice.91
  235.0 6.3 %fusion.14 = f32[8]{0:T(128)S(1)} fusion(bf16[256,8,1536]{2,0,1:T(8,128)(2,1)} %get-tuple-element.307, f32[]{:T(128)} %bitcast.50, f32[8]{0:T(128)S(1)} %get-tuple-element.310, f32[1536,192]{0,1:T(8,128)S(1)} %broadcast_add_fusion.2, bf16[256,8,192]{0,2,1:T(8,128)(2,1)S(1)} %get-tuple-element.306, s32[]{:T(128)} %get-tuple-element.290), kind=kOutput, calls=%fused_computation.1.clone.1 | convolution fusion | flops 1219756032 | bytes 7569960 | tf_op jit(solution)/shard_map/while/body/eval_jaxpr/dot_general | solution.py:10
  241.3 0.6 dynamic_slice.92
  242.6 0.1 dynamic_slice.93
  242.6 0.1 broadcast_add_fusion.2
  242.8 0.6 dynamic_slice.90
  245.3 0.6 dynamic_slice.91
  245.9 6.3 %fusion.14 = f32[8]{0:T(128)S(1)} fusion(bf16[256,8,1536]{2,0,1:T(8,128)(2,1)} %get-tuple-element.307, f32[]{:T(128)} %bitcast.50, f32[8]{0:T(128)S(1)} %get-tuple-element.310, f32[1536,192]{0,1:T(8,128)S(1)} %broadcast_add_fusion.2, bf16[256,8,192]{0,2,1:T(8,128)(2,1)S(1)} %get-tuple-element.306, s32[]{:T(128)} %get-tuple-element.290), kind=kOutput, calls=%fused_computation.1.clone.1 | convolution fusion | flops 1219756032 | bytes 7569960 | tf_op jit(solution)/shard_map/while/body/eval_jaxpr/dot_general | solution.py:10
  252.2 0.6 dynamic_slice.92
  253.5 0.1 dynamic_slice.93
  253.6 0.1 broadcast_add_fusion.2
  253.7 0.6 dynamic_slice.90
  256.2 0.6 dynamic_slice.91
  256.9 6.3 %fusion.14 = f32[8]{0:T(128)S(1)} fusion(bf16[256,8,1536]{2,0,1:T(8,128)(2,1)} %get-tuple-element.307, f32[]{:T(128)} %bitcast.50, f32[8]{0:T(128)S(1)} %get-tuple-element.310, f32[1536,192]{0,1:T(8,128)S(1)} %broadcast_add_fusion.2, bf16[256,8,192]{0,2,1:T(8,128)(2,1)S(1)} %get-tuple-element.306, s32[]{:T(128)} %get-tuple-element.290), kind=kOutput, calls=%fused_computation.1.clone.1 | convolution fusion | flops 1219756032 | bytes 7569960 | tf_op jit(solution)/shard_map/while/body/eval_jaxpr/dot_general | solution.py:10
  263.2 0.6 dynamic_slice.92
  264.4 0.1 dynamic_slice.93
  264.5 0.1 broadcast_add_fusion.2
  264.7 0.6 dynamic_slice.90
  267.2 0.6 dynamic_slice.91
  267.8 6.3 %fusion.14 = f32[8]{0:T(128)S(1)} fusion(bf16[256,8,1536]{2,0,1:T(8,128)(2,1)} %get-tuple-element.307, f32[]{:T(128)} %bitcast.50, f32[8]{0:T(128)S(1)} %get-tuple-element.310, f32[1536,192]{0,1:T(8,128)S(1)} %broadcast_add_fusion.2, bf16[256,8,192]{0,2,1:T(8,128)(2,1)S(1)} %get-tuple-element.306, s32[]{:T(128)} %get-tuple-element.290), kind=kOutput, calls=%fused_computation.1.clone.1 | convolution fusion | flops 1219756032 | bytes 7569960 | tf_op jit(solution)/shard_map/while/body/eval_jaxpr/dot_general | solution.py:10
  274.1 0.6 dynamic_slice.92
  275.4 0.1 dynamic_slice.93
  275.4 0.1 broadcast_add_fusion.2
  275.6 0.6 dynamic_slice.90
  278.1 0.6 dynamic_slice.91
  278.7 6.3 %fusion.14 = f32[8]{0:T(128)S(1)} fusion(bf16[256,8,1536]{2,0,1:T(8,128)(2,1)} %get-tuple-element.307, f32[]{:T(128)} %bitcast.50, f32[8]{0:T(128)S(1)} %get-tuple-element.310, f32[1536,192]{0,1:T(8,128)S(1)} %broadcast_add_fusion.2, bf16[256,8,192]{0,2,1:T(8,128)(2,1)S(1)} %get-tuple-element.306, s32[]{:T(128)} %get-tuple-element.290), kind=kOutput, calls=%fused_computation.1.clone.1 | convolution fusion | flops 1219756032 | bytes 7569960 | tf_op jit(solution)/shard_map/while/body/eval_jaxpr/dot_general | solution.py:10
  285.0 0.7 copy.23
  (28 shorter events, 0.3 us)
Async XLA Ops:
  17.9 2.6 copy-start.1
  26.7 6.8 %copy-start.4 = (s32[8]{0:T(128)S(1)}, s32[8]{0:T(128)}, u32[]{:S(2)}) copy-start(s32[8]{0:T(128)} %param.13) | copy-start | bytes 100
  26.7 12.5 %copy-start.3 = (s32[8]{0:T(128)S(1)}, s32[8]{0:T(128)}, u32[]{:S(2)}) copy-start(s32[8]{0:T(128)} %param.12) | copy-start | bytes 100
  26.7 159.1 %copy-start.5 = (f32[128]{0:T(128)S(1)}, f32[128]{0:T(128)}, u32[]{:S(2)}) copy-start(f32[128]{0:T(128)} %param.10) | copy-start | bytes 1540
  26.8 159.2 %all-to-all-start = ((bf16[16,128,1536]{2,0,1:T(8,128)(2,1)}), bf16[16,128,1536]{2,0,1:T(8,128)(2,1)}, u32[]{:S(2)}, u32[]{:S(2)}) async-start(bf16[16,128,1536]{2,0,1:T(8,128)(2,1)} %copy.19), calls=%async_computation | async-start | bytes 12582912 | tf_op jit(solution)/shard_map/all_to_all | solution.py:35
  192.8 4.7 %copy-start = (bf16[16,16,8,1536]{3,2,1,0:T(8,128)(2,1)}, bf16[16,16,8,1536]{3,2,1,0:T(8,128)(2,1)S(1)}, u32[]{:S(2)}) copy-start(bf16[16,16,8,1536]{3,2,1,0:T(8,128)(2,1)S(1)} %copy.20) | copy-start | bytes 18874372
  192.8 4.7 %copy-start.2 = (f32[1536]{0:T(1024)S(1)}, f32[1536]{0:T(1024)}, u32[]{:S(2)}) copy-start(f32[1536]{0:T(1024)} %param.11) | copy-start | bytes 18436
where the time goes:
time: 287 us; the launch traced here: 286 us
  blocking collectives  128 us (45%)
  matrix products  67.4 us (23%)
  local copies, waits for them, and re-layouts  40.8 us (14%)
  between operations  21.1 us (7%)
  loops' own time  20.6 us (7%)
  starting transfers between devices  6.74 us (2%)
    all_gather x1, blocking collectives, per_device(): blocks = lax.all_gather(pieces, 'occ', axis=0, tiled=True)  128 us
    dot_general x8, matrix products, pair_column(): lax.dot_general(factors, block, (((0,), (0,)), ((), ())), preferred_eleme...  50.1 us
    another operation x1, loops' own time, per_device(): energies = lax.fori_loop(0, step_count, step_body, energies)  20.6 us
    dot_general x1, matrix products, per_device(): jnp.dot(flat, orbitals, preferred_element_type=jnp.float32)  17.3 us
    all_to_all x1, local copies, waits for them, and re-layouts, per_device(): lax.all_to_all(product, 'occ', split_axis=1, concat_axis=0, tiled=True)  6.9 us
    all_to_all x1, starting transfers between devices, per_device(): lax.all_to_all(product, 'occ', split_axis=1, concat_axis=0, tiled=True)  6.74 us
    reshape x1, local copies, waits for them, and re-layouts, per_device(): product = product.reshape(aux_here, occ_total, orbitals.shape[1])  6.2 us
  transfers between devices with their start and end apart: 1, of which 0 were waited for; matrix products, arithmetic and copies ran while one was open for 1% of the time, Pallas kernels for 0%

commit v1 on v0

--- a/solution.py
+++ b/solution.py
@@ -32,7 +32,12 @@
 
     pieces = jnp.stack([own_piece(step) for step in range(step_count)], axis=1)
     blocks = lax.all_gather(pieces, "occ", axis=0, tiled=True)
-    factors = lax.all_to_all(product, "occ", split_axis=1, concat_axis=0, tiled=True)
+    factors = jnp.concatenate(
+        lax.all_to_all(
+            jnp.stack(jnp.split(product, lax.psum(1, "occ"), axis=1), axis=0), "occ", 0, 0
+        ),
+        axis=0,
+    )
     local_count = factors.shape[1]
     occ_here = lax.dynamic_slice(occ_energy, (lax.axis_index("occ") * local_count,), (local_count,))
     energies = jnp.zeros((local_count, step_count), jnp.float32)

time: 287 us -> 292 us (1.017)
  local copies, waits for them, and re-layouts: 40.8 us -> 46.5 us
    unnamed x13 -> x27, local copies, waits for them, and re-layouts: 3.32 us -> 18.9 us
    all_to_all x1 -> x0, local copies, waits for them, and re-layouts: 6.9 us -> none  [per_device(): lax.all_to_all(product, 'occ', split_axis=1, concat_axis=0, tiled=True)]
    reshape x1 -> x0, local copies, waits for them, and re-layouts: 6.2 us -> none  [per_device(): product = product.reshape(aux_here, occ_total, orbitals.shape[1])]
where the time goes in v1:
time: 292 us; the launch traced here: 291 us
  blocking collectives  128 us (44%)
  matrix products  67.3 us (23%)
  local copies, waits for them, and re-layouts  46.5 us (16%)
  between operations  21.1 us (7%)
  loops' own time  20.1 us (7%)
  starting transfers between devices  6.74 us (2%)
    all_gather x1, blocking collectives, per_device(): blocks = lax.all_gather(pieces, 'occ', axis=0, tiled=True)  128 us
    dot_general x8, matrix products, pair_column(): lax.dot_general(factors, block, (((0,), (0,)), ((), ())), preferred_eleme...  50 us
    another operation x1, loops' own time, per_device(): energies = lax.fori_loop(0, step_count, step_body, energies)  20.1 us
    unnamed x27, local copies, waits for them, and re-layouts  18.9 us
    dot_general x1, matrix products, per_device(): jnp.dot(flat, orbitals, preferred_element_type=jnp.float32)  17.3 us
    while x2, local copies, waits for them, and re-layouts, per_device(): energies = lax.fori_loop(0, step_count, step_body, energies)  8.51 us
    all_to_all x1, starting transfers between devices, per_device(): lax.all_to_all(jnp.stack(jnp.split(product, lax.psum(1, 'occ'), axis=1),...  6.74 us
  transfers between devices with their start and end apart: 1, of which 0 were waited for; matrix products, arithmetic and copies ran while one was open for 1% of the time, Pallas kernels for 0%

profile of v1, /device:TPU:9, one launch (start us, length us, event | category | flops | bytes accessed | tf_op | source)
XLA Modules:
  0.0 290.7 jit_solution(9168520508391145790)
XLA Ops:
  0.6 17.3 %convolution_convert_fusion = bf16[2048,1536]{1,0:T(8,128)(2,1)S(1)} fusion(bf16[2048,2048]{1,0:T(8,128)(2,1)} %bitcast.130, bf16[2048,1536]{1,0:T(8,128)(2,1)} %param.9), kind=kOutput, calls=%fused_computation.7 | convolution fusion | flops 12888047616 | bytes 20971520 | tf_op jit(solution)/shard_map/dot_general | solution.py:24
  17.9 0.8 fusion.19
  18.8 1.3 fusion.18
  20.1 0.9 fusion.17
  21.0 0.8 fusion.16
  21.7 0.8 fusion.15
  22.5 0.8 fusion.14
  23.3 0.8 fusion.13
  24.0 0.8 fusion.12
  24.8 0.8 fusion.11
  25.6 0.8 fusion.10
  26.4 0.8 fusion.9
  27.1 0.8 fusion.8
  27.9 0.8 fusion.7
  28.7 0.8 fusion.6
  29.5 0.8 fusion.5
  30.2 0.8 fusion.4
  31.0 6.7 %all-to-all-start = ((bf16[16,16,8,1536]{3,2,1,0:T(8,128)(2,1)}), bf16[16,16,8,1536]{3,2,1,0:T(8,128)(2,1)}, u32[]{:S(2)}, u32[]{:S(2)}) async-start(bf16[16,16,8,1536]{3,2,1,0:T(8,128)(2,1)} %fusion.4), calls=%async_computation | async-start | bytes 12582912 | tf_op jit(solution)/shard_map/all_to_all | solution.py:36
  37.8 0.7 fusion.20
  43.5 0.7 fusion.21
  59.6 1.5 constant_dynamic-slice_fusion
  61.1 0.2 stack.71
  61.3 127.8 %all_gather.3 = bf16[256,8,192]{2,1,0:T(8,128)(2,1)S(1)} all-gather(bf16[16,8,192]{2,1,0:T(8,128)(2,1)S(1)} %stack.71), channel_id=1, replica_groups=mesh['mol'=2,'occ'=16] {'occ'}, dimensions={0}, use_global_device_ids=true | all-gather | bytes 835584 | tf_op jit(solution)/shard_map/all_gather | solution.py:34
  189.1 1.0 copy.18
  190.2 7.5 %copy.19 = bf16[256,8,1536]{2,0,1:T(8,128)(2,1)} copy(bf16[256,8,1536]{2,1,0:T(8,128)(2,1)} %bitcast.25) | data formatting | bytes 12582912 | tf_op jit(solution)/shard_map/while | solution.py:52
  197.7 86.4 %while.13 = (s32[]{:T(128)}, f32[8,8]{0,1:T(8,128)S(1)}, bf16[256,8,192]{0,2,1:T(8,128)(2,1)S(1)}, bf16[256,8,1536]{2,0,1:T(8,128)(2,1)}, f32[1536]{0:T(1024)S(1...) while((s32[]{:T(128)}, f32[8,8]{0,1:T(8,128)S(1)}, ...), condition=%wide.region_2.3_spmd, body=%wide.region_0.2_spmd.sunk | while | flops 1220050944 | bytes 8758441 | solution.py:52
  197.7 0.6 dynamic_slice.92
  199.0 0.1 broadcast_add_fusion.2
  199.2 0.6 dynamic_slice.90
  201.6 0.6 dynamic_slice.91
  202.2 6.2 %fusion.30 = f32[8]{0:T(128)S(1)} fusion(bf16[256,8,1536]{2,0,1:T(8,128)(2,1)} %get-tuple-element.307, f32[]{:T(128)} %bitcast.111, f32[8]{0:T(128)S(1)} %get-tuple-element.310, f32[1536,192]{0,1:T(8,128)S(1)} %broadcast_add_fusion.2, bf16[256,8,192]{0,2,1:T(8,128)(2,1)S(1)} %get-tuple-element.306, s32[]{:T(128)} %get-tuple-element.290), kind=kOutput, calls=%fused_computation.1.clone.1 | convolution fusion | flops 1219756032 | bytes 7569960 | tf_op jit(solution)/shard_map/while/body/eval_jaxpr/dot_general | solution.py:10
  208.5 0.6 dynamic_slice.92
  209.8 0.1 broadcast_add_fusion.2
  210.0 0.6 dynamic_slice.90
  212.4 0.6 dynamic_slice.91
  213.0 6.2 %fusion.30 = f32[8]{0:T(128)S(1)} fusion(bf16[256,8,1536]{2,0,1:T(8,128)(2,1)} %get-tuple-element.307, f32[]{:T(128)} %bitcast.111, f32[8]{0:T(128)S(1)} %get-tuple-element.310, f32[1536,192]{0,1:T(8,128)S(1)} %broadcast_add_fusion.2, bf16[256,8,192]{0,2,1:T(8,128)(2,1)S(1)} %get-tuple-element.306, s32[]{:T(128)} %get-tuple-element.290), kind=kOutput, calls=%fused_computation.1.clone.1 | convolution fusion | flops 1219756032 | bytes 7569960 | tf_op jit(solution)/shard_map/while/body/eval_jaxpr/dot_general | solution.py:10
  219.3 0.6 dynamic_slice.92
  220.6 0.1 broadcast_add_fusion.2
  220.8 0.6 dynamic_slice.90
  223.2 0.6 dynamic_slice.91
  223.8 6.2 %fusion.30 = f32[8]{0:T(128)S(1)} fusion(bf16[256,8,1536]{2,0,1:T(8,128)(2,1)} %get-tuple-element.307, f32[]{:T(128)} %bitcast.111, f32[8]{0:T(128)S(1)} %get-tuple-element.310, f32[1536,192]{0,1:T(8,128)S(1)} %broadcast_add_fusion.2, bf16[256,8,192]{0,2,1:T(8,128)(2,1)S(1)} %get-tuple-element.306, s32[]{:T(128)} %get-tuple-element.290), kind=kOutput, calls=%fused_computation.1.clone.1 | convolution fusion | flops 1219756032 | bytes 7569960 | tf_op jit(solution)/shard_map/while/body/eval_jaxpr/dot_general | solution.py:10
  230.1 0.6 dynamic_slice.92
  231.4 0.1 broadcast_add_fusion.2
  231.6 0.6 dynamic_slice.90
  234.0 0.6 dynamic_slice.91
  234.6 6.2 %fusion.30 = f32[8]{0:T(128)S(1)} fusion(bf16[256,8,1536]{2,0,1:T(8,128)(2,1)} %get-tuple-element.307, f32[]{:T(128)} %bitcast.111, f32[8]{0:T(128)S(1)} %get-tuple-element.310, f32[1536,192]{0,1:T(8,128)S(1)} %broadcast_add_fusion.2, bf16[256,8,192]{0,2,1:T(8,128)(2,1)S(1)} %get-tuple-element.306, s32[]{:T(128)} %get-tuple-element.290), kind=kOutput, calls=%fused_computation.1.clone.1 | convolution fusion | flops 1219756032 | bytes 7569960 | tf_op jit(solution)/shard_map/while/body/eval_jaxpr/dot_general | solution.py:10
  240.9 0.6 dynamic_slice.92
  242.4 0.6 dynamic_slice.90
  244.8 0.6 dynamic_slice.91
  245.4 6.2 %fusion.30 = f32[8]{0:T(128)S(1)} fusion(bf16[256,8,1536]{2,0,1:T(8,128)(2,1)} %get-tuple-element.307, f32[]{:T(128)} %bitcast.111, f32[8]{0:T(128)S(1)} %get-tuple-element.310, f32[1536,192]{0,1:T(8,128)S(1)} %broadcast_add_fusion.2, bf16[256,8,192]{0,2,1:T(8,128)(2,1)S(1)} %get-tuple-element.306, s32[]{:T(128)} %get-tuple-element.290), kind=kOutput, calls=%fused_computation.1.clone.1 | convolution fusion | flops 1219756032 | bytes 7569960 | tf_op jit(solution)/shard_map/while/body/eval_jaxpr/dot_general | solution.py:10
  251.7 0.6 dynamic_slice.92
  253.2 0.6 dynamic_slice.90
  255.6 0.6 dynamic_slice.91
  256.2 6.2 %fusion.30 = f32[8]{0:T(128)S(1)} fusion(bf16[256,8,1536]{2,0,1:T(8,128)(2,1)} %get-tuple-element.307, f32[]{:T(128)} %bitcast.111, f32[8]{0:T(128)S(1)} %get-tuple-element.310, f32[1536,192]{0,1:T(8,128)S(1)} %broadcast_add_fusion.2, bf16[256,8,192]{0,2,1:T(8,128)(2,1)S(1)} %get-tuple-element.306, s32[]{:T(128)} %get-tuple-element.290), kind=kOutput, calls=%fused_computation.1.clone.1 | convolution fusion | flops 1219756032 | bytes 7569960 | tf_op jit(solution)/shard_map/while/body/eval_jaxpr/dot_general | solution.py:10
  262.5 0.6 dynamic_slice.92
  264.0 0.6 dynamic_slice.90
  266.5 0.6 dynamic_slice.91
  267.0 6.2 %fusion.30 = f32[8]{0:T(128)S(1)} fusion(bf16[256,8,1536]{2,0,1:T(8,128)(2,1)} %get-tuple-element.307, f32[]{:T(128)} %bitcast.111, f32[8]{0:T(128)S(1)} %get-tuple-element.310, f32[1536,192]{0,1:T(8,128)S(1)} %broadcast_add_fusion.2, bf16[256,8,192]{0,2,1:T(8,128)(2,1)S(1)} %get-tuple-element.306, s32[]{:T(128)} %get-tuple-element.290), kind=kOutput, calls=%fused_computation.1.clone.1 | convolution fusion | flops 1219756032 | bytes 7569960 | tf_op jit(solution)/shard_map/while/body/eval_jaxpr/dot_general | solution.py:10
  273.3 0.6 dynamic_slice.92
  274.8 0.6 dynamic_slice.90
  277.3 0.6 dynamic_slice.91
  277.9 6.2 %fusion.30 = f32[8]{0:T(128)S(1)} fusion(bf16[256,8,1536]{2,0,1:T(8,128)(2,1)} %get-tuple-element.307, f32[]{:T(128)} %bitcast.111, f32[8]{0:T(128)S(1)} %get-tuple-element.310, f32[1536,192]{0,1:T(8,128)S(1)} %broadcast_add_fusion.2, bf16[256,8,192]{0,2,1:T(8,128)(2,1)S(1)} %get-tuple-element.306, s32[]{:T(128)} %get-tuple-element.290), kind=kOutput, calls=%fused_computation.1.clone.1 | convolution fusion | flops 1219756032 | bytes 7569960 | tf_op jit(solution)/shard_map/while/body/eval_jaxpr/dot_general | solution.py:10
  284.1 0.7 copy.20
  284.8 5.9 %copy.44 = bf16[256,8,1536]{2,1,0:T(8,128)(2,1)} copy(bf16[256,8,1536]{2,1,0:T(8,128)(2,1)} %bitcast.25) | data formatting | bytes 12582912
  (41 shorter events, 1.6 us)
Async XLA Ops:
  17.9 12.3 %copy-start = (bf16[2048,1536]{1,0:T(8,128)(2,1)}, bf16[2048,1536]{1,0:T(8,128)(2,1)S(1)}, u32[]{:S(2)}) copy-start(bf16[2048,1536]{1,0:T(8,128)(2,1)S(1)} %convolution_convert_fusion) | copy-start | bytes 18874372
  31.0 6.8 %copy-start.3 = (s32[8]{0:T(128)S(1)}, s32[8]{0:T(128)}, u32[]{:S(2)}) copy-start(s32[8]{0:T(128)} %param.13) | copy-start | bytes 100
  31.0 12.5 %copy-start.2 = (s32[8]{0:T(128)S(1)}, s32[8]{0:T(128)}, u32[]{:S(2)}) copy-start(s32[8]{0:T(128)} %param.12) | copy-start | bytes 100
  31.0 159.1 %copy-start.4 = (f32[128]{0:T(128)S(1)}, f32[128]{0:T(128)}, u32[]{:S(2)}) copy-start(f32[128]{0:T(128)} %param.10) | copy-start | bytes 1540
  31.0 159.2 %all-to-all-start = ((bf16[16,16,8,1536]{3,2,1,0:T(8,128)(2,1)}), bf16[16,16,8,1536]{3,2,1,0:T(8,128)(2,1)}, u32[]{:S(2)}, u32[]{:S(2)}) async-start(bf16[16,16,8,1536]{3,2,1,0:T(8,128)(2,1)} %fusion.4), calls=%async_computation | async-start | bytes 12582912 | tf_op jit(solution)/shard_map/all_to_all | solution.py:36
  190.2 7.5 %copy-start.1 = (f32[1536]{0:T(1024)S(1)}, f32[1536]{0:T(1024)}, u32[]{:S(2)}) copy-start(f32[1536]{0:T(1024)} %param.11) | copy-start | bytes 18436
